TPU v7x, 512 devices: a whole 4x4x16 slice. The times are simulated.
512 devices in a mesh: pipe: 4 (over y), expert: 32 (over z, core), tensor: 4 (over x).
Axes of the slice: x: 4, y: 4, z: 16, core: 2. Of those that a mesh axis runs over, the one named last changes fastest.
Arguments:
- tokens: bfloat16 [512, 6144], P('expert', ('pipe', 'tensor')), may hold values from -6 to 6
- expert_ids: int32 [512, 2], P('expert'), may hold values from 0 to 7, all different within a row; in each aligned block of 16 rows (0 to 15, 16 to 31, ...) at most 5 rows name the same one
- gates: float32 [512, 2], P('expert'), may hold values from 0.2 to 1
- w_gate: bfloat16 [32, 6144, 2048], P('expert', None, ('pipe', 'tensor')), may hold values from -0.078125 to 0.078125
- w_up: bfloat16 [32, 6144, 2048], P('expert', None, ('pipe', 'tensor')), may hold values from -0.078125 to 0.078125
- w_down: bfloat16 [32, 2048, 6144], P('expert', ('pipe', 'tensor')), may hold values from -0.0625 to 0.0625
- d_out: bfloat16 [512, 6144], P('expert', ('pipe', 'tensor')), may hold values from -6 to 6
Outputs:
- moe_out: bfloat16 [512, 6144], P('expert', ('pipe', 'tensor'))
- grad_tokens: bfloat16 [512, 6144], P('expert', ('pipe', 'tensor'))
- grad_gates: float32 [512, 2], P('expert')
Inputs may be any that keep to these rules, and one draw needn't show every extreme that they name: `expert_ids`: each row names 2 different experts. Among the rows of one index of expert (aligned blocks of 16 rows) no expert is named more than 5 times, a bound that some block reaches.
All inputs are finite; a program needn't handle non-finite values.
Results may differ from a plain program's by a relative error of at most 0.017.
Values may be sent and summed in bfloat16 or wider, within the bound.
No kernel may reach another device: no remote copies, remote signals or barrier semaphores. Data moves between devices by JAX's collectives and lax.ppermute only.
A program may use at most 64 MiB of HBM per device.

v0:
```python
import jax
import jax.numpy as jnp
from jax import lax
from jax.sharding import PartitionSpec as P


def per_device(tokens, expert_ids, gates, w_gate, w_up, w_down, d_out):
    tok_rows = tokens.shape[0]
    feat = tokens.shape[1]
    top = expert_ids.shape[1]
    devices_all = lax.axis_size("expert")
    experts = min(8, devices_all)
    group = devices_all // experts
    capacity = min(
        tok_rows,
        max(2, max(5 * tok_rows * top // (4 * experts), (tok_rows * top + experts - 1) // experts)),
    )
    slots = experts * capacity
    flat_ids = expert_ids.reshape(-1)
    onehot = (flat_ids[:, None] == jnp.arange(experts, dtype=jnp.int32)[None, :]).astype(jnp.int32)
    position = jnp.sum(jnp.cumsum(onehot, axis=0) * onehot, axis=1) - 1
    slot_of = flat_ids * capacity + position
    picks = (jnp.arange(slots, dtype=jnp.int32)[:, None] == slot_of[None, :]).astype(jnp.float32)
    pick_rows = picks.reshape(slots, tok_rows, top)
    select_tok = jnp.sum(pick_rows, axis=2).astype(jnp.bfloat16)
    select_gate = jnp.sum(pick_rows * gates[None, :, :], axis=2)
    picked = jnp.dot(select_tok, tokens, preferred_element_type=jnp.float32).astype(jnp.bfloat16)
    scaled = jnp.dot(
        select_gate, d_out.astype(jnp.float32), precision=lax.Precision.HIGHEST
    ).astype(jnp.bfloat16)
    send = jnp.concatenate([picked, scaled], axis=1).reshape(experts, capacity, 2 * feat)
    send = jnp.repeat(send, group, axis=0)
    recv = lax.all_to_all(send, "expert", split_axis=0, concat_axis=0, tiled=True)
    recv = recv.reshape(devices_all * capacity, 2 * feat)
    part_x = recv[:, :feat]
    part_dy = recv[:, feat:]
    rows_x = lax.all_gather(part_x, ("pipe", "tensor"), axis=1, tiled=True)
    rows_dy = lax.all_gather(part_dy, ("pipe", "tensor"), axis=1, tiled=True)
    gate_proj = w_gate[0]
    up_proj = w_up[0]
    down_proj = w_down[0]
    contract_last = (((1,), (1,)), ((), ()))
    h_gate = jnp.dot(rows_x, gate_proj, preferred_element_type=jnp.float32)
    h_up = jnp.dot(rows_x, up_proj, preferred_element_type=jnp.float32)
    sig = jax.nn.sigmoid(h_gate)
    hidden = (h_gate * sig * h_up).astype(jnp.bfloat16)
    out_terms = jnp.dot(hidden, down_proj, preferred_element_type=jnp.float32)
    d_hidden = lax.dot_general(
        rows_dy, down_proj, contract_last, preferred_element_type=jnp.float32
    )
    d_gate_h = (d_hidden * h_up * sig * (1.0 + h_gate * (1.0 - sig))).astype(jnp.bfloat16)
    d_up_h = (d_hidden * h_gate * sig).astype(jnp.bfloat16)
    dx_terms = lax.dot_general(
        d_gate_h, gate_proj, contract_last, preferred_element_type=jnp.float32
    )
    dx_terms = dx_terms + lax.dot_general(
        d_up_h, up_proj, contract_last, preferred_element_type=jnp.float32
    )
    out_share = lax.psum_scatter(
        out_terms.astype(jnp.bfloat16), ("pipe", "tensor"), scatter_dimension=1, tiled=True
    )
    dx_share = lax.psum_scatter(
        dx_terms.astype(jnp.bfloat16), ("pipe", "tensor"), scatter_dimension=1, tiled=True
    )
    back_send = jnp.concatenate([out_share, dx_share], axis=1).reshape(
        devices_all, capacity, 2 * feat
    )
    back = lax.all_to_all(back_send, "expert", split_axis=0, concat_axis=0, tiled=True)
    back_rows = (
        jnp.sum(back.astype(jnp.float32).reshape(experts, group, capacity, 2 * feat), axis=1)
        .astype(jnp.bfloat16)
        .reshape(slots, 2 * feat)
    )
    assign = picks.T.astype(jnp.bfloat16)
    a_both = jnp.dot(assign, back_rows, preferred_element_type=jnp.float32)
    a_out = a_both[:, :feat].reshape(tok_rows, top, feat)
    a_dx = a_both[:, feat:].reshape(tok_rows, top, feat)
    moe_out = jnp.sum(gates[:, :, None] * a_out, axis=1).astype(jnp.bfloat16)
    grad_tokens = jnp.sum(a_dx, axis=1).astype(jnp.bfloat16)
    partial_dots = jnp.sum(d_out.astype(jnp.float32)[:, None, :] * a_out, axis=2)
    grad_gates = lax.psum(partial_dots, ("pipe", "tensor"))
    return (moe_out, grad_tokens, grad_gates)


def solution(mesh):
    return jax.shard_map(
        per_device,
        mesh=mesh,
        in_specs=(
            P("expert", ("pipe", "tensor")),
            P("expert", None),
            P("expert", None),
            P("expert", None, ("pipe", "tensor")),
            P("expert", None, ("pipe", "tensor")),
            P("expert", ("pipe", "tensor"), None),
            P("expert", ("pipe", "tensor")),
        ),
        out_specs=(
            P("expert", ("pipe", "tensor")),
            P("expert", ("pipe", "tensor")),
            P("expert", None),
        ),
        check_vma=False,
    )
```

profile of v0, /device:TPU:32, one launch (start us, length us, event | category | flops | bytes accessed | tf_op | source)
XLA Modules:
  0.0 457.4 jit_solution(14242704866884179317)
XLA Ops:
  7.2 0.0 copy-start
  7.2 0.0 all-gather.3.cloned.1.call-start
  7.2 0.9 copy.35
  8.1 0.1 reshape.63
  8.2 0.1 fusion.14
  8.3 0.1 reduce_window_sum.11
  8.3 0.2 select_reduce_fusion.1
  8.5 0.1 sub.10
  8.6 0.1 copy.36
  8.7 0.7 multiply_add_fusion
  9.4 0.8 convert_reduce_fusion
  10.1 0.9 convolution_convert_fusion.1
  11.1 0.9 convolution_convert_fusion.2
  12.1 41.8 %all_to_all.10 = bf16[32,5,768]{2,1,0:T(8,128)(2,1)S(1)} all-to-all(bf16[32,5,768]{2,1,0:T(8,128)(2,1)S(1)} %bitcast.32), channel_id=1, replica_groups=mesh['pipe'=4,'expert'=32,'tensor'=4] {'expert'}, dimensions={0} | all-to-all | bytes 491520 | tf_op jit(solution)/shard_map/all_to_all | solution.py:33
  53.9 0.1 reshape.66
  54.0 0.7 fusion.21
  54.7 0.0 all-gather.3.cloned.1.call-update
  54.8 0.0 all-gather.5.cloned.1.call-start
  54.8 0.7 all-gather.5.cloned.1.call-update
  55.5 0.0 reduce-scatter.9.cloned.1.call-start
  55.6 54.5 %all-gather.3.cloned.1.call-done = bf16[160,6144]{1,0:T(8,128)(2,1)} async-done(((bf16[160,384]{1,0:T(8,128)(2,1)}), bf16[160,6144]{1,0:T(8,128)(2,1)}) %all-gather.3.cloned.1.call-update) | async-done | bytes 1966096 | tf_op jit(solution)/shard_map/all_gather | solution.py:37
  110.0 0.0 copy-done
  110.0 0.0 copy-start.1
  110.0 2.3 fusion.9
  112.4 0.0 copy-done.1
  112.4 0.0 copy-start.4
  112.4 0.0 copy-start.2
  112.4 2.2 fusion.5
  114.6 0.0 copy-start.5
  114.6 60.3 %all-gather.5.cloned.1.call-done = bf16[160,6144]{1,0:T(8,128)(2,1)} async-done(((bf16[160,384]{1,0:T(8,128)(2,1)}), bf16[160,6144]{1,0:T(8,128)(2,1)}) %all-gather.5.cloned.1.call-update) | async-done | bytes 1966096 | tf_op jit(solution)/shard_map/all_gather | solution.py:38
  174.9 0.0 copy-done.2
  174.9 2.2 fusion.1
  177.1 0.0 copy-done.4
  177.1 0.0 copy-done.5
  177.1 0.0 copy-start.3
  177.1 0.7 fusion.7
  177.8 0.7 copy-done.3
  178.5 1.6 fusion
  180.1 2.8 copy.40
  182.9 0.0 reduce-scatter.9.cloned.1.call-update
  182.9 0.0 reduce-scatter.7.cloned.1.call-start
  182.9 2.2 convolution_convert_fusion
  185.1 2.8 copy.38
  187.9 0.0 reduce-scatter.7.cloned.1.call-update
  187.9 0.0 copy-start.7
  187.9 0.0 copy-start.6
  187.9 85.6 %reduce-scatter.9.cloned.1.call-done = bf16[384,160]{1,0:T(8,128)(2,1)} async-done(((bf16[6144,160]{1,0:T(8,128)(2,1)}), bf16[384,160]{1,0:T(8,128)(2,1)}) %reduce-scatter.9.cloned.1.call-update) | async-done | bytes 122896
  273.6 1.1 copy.41
  274.6 93.5 %reduce-scatter.7.cloned.1.call-done = bf16[384,160]{1,0:T(8,128)(2,1)} async-done(((bf16[6144,160]{1,0:T(8,128)(2,1)}), bf16[384,160]{1,0:T(8,128)(2,1)}) %reduce-scatter.7.cloned.1.call-update) | async-done | bytes 122896
  368.1 1.1 copy.39
  369.2 0.8 reshape.67
  370.1 12.8 %all-to-all-start.1 = ((bf16[32,5,768]{2,1,0:T(8,128)(2,1)}), bf16[32,5,768]{2,1,0:T(8,128)(2,1)S(1)}, u32[]{:S(2)}, u32[]{:S(2)}) async-start(bf16[32,5,768]{2,1,0:T(8,128)(2,1)} %reshape.67), calls=%async_computation.1 | async-start | bytes 786432 | tf_op jit(solution)/shard_map/all_to_all | solution.py:68
  382.9 0.0 copy-done.7
  382.9 0.1 copy.34
  383.0 0.0 copy-done.6
  383.0 26.5 %all-to-all-done.1 = bf16[32,5,768]{2,1,0:T(8,128)(2,1)S(1)} async-done(((bf16[32,5,768]{2,1,0:T(8,128)(2,1)}), bf16[32,5,768]{2,1,0:T(8,128)(2,1)S(1)}, u32[]{:S(2)}, u32[]{:S(2)}) %all-to-all-start.1) | async-done | bytes 245792 | tf_op jit(solution)/shard_map/all_to_all | solution.py:68
  409.6 0.1 bitcast_reduce_fusion
  409.7 0.2 fusion.15
  409.9 0.1 multiply_reduce_fusion
  410.1 0.1 reduce_sum.72
  410.2 38.6 %psum.7 = f32[16,2]{1,0:T(8,128)S(1)} all-reduce(f32[16,2]{1,0:T(8,128)S(1)} %reduce_sum.72), channel_id=1, replica_groups=mesh['pipe'=4,'expert'=32,'tensor'=4] {'pipe','tensor'}, use_global_device_ids=true, to_apply=%region_10.11 | all-reduce | flops 32 | bytes 256 | tf_op jit(solution)/shard_map/psum | solution.py:81
  448.8 0.6 copy.37
  449.5 0.7 multiply_reduce_fusion.1
  450.2 0.7 reduce_sum.70
  (10 shorter events, 0.2 us)
Async XLA Ops:
  7.2 102.9 %copy-start = (bf16[1,6144,128]{2,1,0:T(8,128)(2,1)S(1)}, bf16[1,6144,128]{2,1,0:T(8,128)(2,1)}, u32[]{:S(2)}) copy-start(bf16[1,6144,128]{2,1,0:T(8,128)(2,1)} %param.10) | copy-start | bytes 4718596
  7.2 102.8 %all-gather.3.cloned.1.call-start = ((), (), s32[]{:S(2)}) async-start(), calls=%async_computation.4 | async-start | bytes 2088960 | tf_op jit(solution)/shard_map/all_gather | solution.py:37
  54.8 120.1 %all-gather.5.cloned.1.call-start = ((), (), s32[]{:S(2)}) async-start(), calls=%async_computation.5 | async-start | bytes 2088960 | tf_op jit(solution)/shard_map/all_gather | solution.py:38
  55.5 218.1 %reduce-scatter.9.cloned.1.call-start = ((), (), s32[]{:S(2)}) async-start(), calls=%async_computation.7 | async-start | bytes 3342336
  110.0 2.4 copy-start.1
  112.4 64.7 %copy-start.4 = (f32[160,128]{1,0:T(8,128)}, f32[160,128]{1,0:T(8,128)S(1)}, u32[]{:S(2)}) copy-start(f32[160,128]{1,0:T(8,128)S(1)} %fusion.9) | copy-start | bytes 245764
  112.4 62.5 %copy-start.2 = (bf16[1,128,6144]{2,1,0:T(8,128)(2,1)S(1)}, bf16[1,128,6144]{2,1,0:T(8,128)(2,1)}, u32[]{:S(2)}) copy-start(bf16[1,128,6144]{2,1,0:T(8,128)(2,1)} %param.12) | copy-start | bytes 4718596
  114.6 62.5 %copy-start.5 = (f32[160,128]{1,0:T(8,128)}, f32[160,128]{1,0:T(8,128)S(1)}, u32[]{:S(2)}) copy-start(f32[160,128]{1,0:T(8,128)S(1)} %fusion.5) | copy-start | bytes 245764
  177.1 1.4 copy-start.3
  182.9 185.2 %reduce-scatter.7.cloned.1.call-start = ((), (), s32[]{:S(2)}) async-start(), calls=%async_computation.6 | async-start | bytes 3342336
  187.9 195.0 %copy-start.7 = (f32[16,2]{0,1:T(2,128)S(1)}, f32[16,2]{0,1:T(2,128)}, u32[]{:S(2)}) copy-start(f32[16,2]{0,1:T(2,128)} %param.9) | copy-start | bytes 388
  187.9 195.1 %copy-start.6 = (bf16[16,384]{1,0:T(8,128)(2,1)S(1)}, bf16[16,384]{1,0:T(8,128)(2,1)}, u32[]{:S(2)}) copy-start(bf16[16,384]{1,0:T(8,128)(2,1)} %param.13) | copy-start | bytes 36868
  370.1 39.5 %all-to-all-start.1 = ((bf16[32,5,768]{2,1,0:T(8,128)(2,1)}), bf16[32,5,768]{2,1,0:T(8,128)(2,1)S(1)}, u32[]{:S(2)}, u32[]{:S(2)}) async-start(bf16[32,5,768]{2,1,0:T(8,128)(2,1)} %reshape.67), calls=%async_computation.1 | async-start | bytes 786432 | tf_op jit(solution)/shard_map/all_to_all | solution.py:68
Sparse Core Ops, SparseCore 0:
  54.9 55.0 all-gather.2
  113.0 61.8 all-gather.4
  183.0 90.5 reduce-scatter.8
  277.6 90.4 reduce-scatter.6
where the time goes:
time: 458 us; the launch traced here: 457 us
  waiting for transfers between devices  321 us (70%)
  blocking collectives  80.5 us (18%)
  between operations  14 us (3%)
  matrix products  13.2 us (3%)
  starting transfers between devices  13 us (3%)
  local copies, waits for them, and re-layouts  12.2 us (3%)
    unnamed x6, waiting for transfers between devices  180 us
    all_gather x1, waiting for transfers between devices, per_device(): rows_dy = lax.all_gather(part_dy, ('pipe', 'tensor'), axis=1, tiled=True)  60.3 us
    all_gather x1, waiting for transfers between devices, per_device(): rows_x = lax.all_gather(part_x, ('pipe', 'tensor'), axis=1, tiled=True)  54.5 us
    all_to_all x1, blocking collectives, per_device(): lax.all_to_all(send, 'expert', split_axis=0, concat_axis=0, tiled=True)  41.8 us
    psum x1, blocking collectives, per_device(): grad_gates = lax.psum(partial_dots, ('pipe', 'tensor'))  38.6 us
    all_to_all x1, waiting for transfers between devices, per_device(): lax.all_to_all(back_send, 'expert', split_axis=0, concat_axis=0, tiled=True)  26.5 us
    all_to_all x1, starting transfers between devices, per_device(): lax.all_to_all(back_send, 'expert', split_axis=0, concat_axis=0, tiled=True)  12.8 us
    unnamed x23, local copies, waits for them, and re-layouts  9.97 us
  transfers between devices with their start and end apart: 5, of which 5 were waited for; matrix products, arithmetic and copies ran while one was open for 2% of the time, Pallas kernels for 0%

commit v1 on v0

--- a/solution.py
+++ b/solution.py
@@ -2,6 +2,24 @@
 import jax.numpy as jnp
 from jax import lax
 from jax.sharding import PartitionSpec as P
+
+
+def ring_gather(shard, axis, dim):
+    ways, here, step = (lax.axis_size(axis), lax.axis_index(axis), shard.shape[dim])
+    lengths = [n * ways if d == dim else n for d, n in enumerate(shard.shape)]
+    full = lax.dynamic_update_slice_in_dim(
+        jnp.zeros(lengths, shard.dtype), shard, here * step, axis=dim
+    )
+    going_up = going_down = shard
+    for far in range(1, ways // 2 + 1):
+        going_up = lax.ppermute(going_up, axis, [(d, (d + 1) % ways) for d in range(ways)])
+        full = lax.dynamic_update_slice_in_dim(full, going_up, (here - far) % ways * step, axis=dim)
+        if 2 * far < ways:
+            going_down = lax.ppermute(going_down, axis, [(d, (d - 1) % ways) for d in range(ways)])
+            full = lax.dynamic_update_slice_in_dim(
+                full, going_down, (here + far) % ways * step, axis=dim
+            )
+    return full
 
 
 def per_device(tokens, expert_ids, gates, w_gate, w_up, w_down, d_out):
@@ -34,7 +52,7 @@
     recv = recv.reshape(devices_all * capacity, 2 * feat)
     part_x = recv[:, :feat]
     part_dy = recv[:, feat:]
-    rows_x = lax.all_gather(part_x, ("pipe", "tensor"), axis=1, tiled=True)
+    rows_x = ring_gather(part_x, ("pipe", "tensor"), 1)
     rows_dy = lax.all_gather(part_dy, ("pipe", "tensor"), axis=1, tiled=True)
     gate_proj = w_gate[0]
     up_proj = w_up[0]

time: 458 us -> 414 us (0.904)
  waiting for transfers between devices: 321 us -> 235 us
  starting transfers between devices: 13 us -> 95.7 us
  blocking collectives: 80.5 us -> 38.7 us
  matrix products: 13.2 us -> 7.68 us
  local copies, waits for them, and re-layouts: 12.2 us -> 17.4 us
    ppermute x0 -> x15, starting transfers between devices: none -> 67.4 us  [the longest x7 50.6 us: ring_gather(): lax.ppermute(going_down, axis, [(d, (d - 1) % ways) for d in range(ways)])]
    all_gather x1, waiting for transfers between devices: 60.3 us -> 0.02 us  [per_device(): rows_dy = lax.all_gather(part_dy, ('pipe', 'tensor'), axis=1, tiled=True)]
    all_gather x1 -> x0, waiting for transfers between devices: 54.5 us -> none  [per_device(): rows_x = lax.all_gather(part_x, ('pipe', 'tensor'), axis=1, tiled=True)]
    all_to_all x1 -> x0, blocking collectives: 41.8 us -> none  [per_device(): lax.all_to_all(send, 'expert', split_axis=0, concat_axis=0, tiled=True)]
    all_to_all x0 -> x1, waiting for transfers between devices: none -> 26.6 us  [per_device(): lax.all_to_all(send, 'expert', split_axis=0, concat_axis=0, tiled=True)]
    all_to_all x0 -> x1, starting transfers between devices: none -> 15.3 us  [per_device(): lax.all_to_all(send, 'expert', split_axis=0, concat_axis=0, tiled=True)]
    ppermute x0 -> x15, waiting for transfers between devices: none -> 13.4 us  [the longest x8 12.5 us: ring_gather(): lax.ppermute(going_up, axis, [(d, (d + 1) % ways) for d in range(ways)])]
    unnamed x6 -> x5, waiting for transfers between devices: 180 us -> 169 us
  transfers between devices with their start and end apart: 5 -> 20, of which waited for: 5 -> 15; matrix products, arithmetic and copies ran while one was open for 2% -> 4% of each run, Pallas kernels for 0% -> 0%
where the time goes in v1:
time: 414 us; the launch traced here: 413 us
  waiting for transfers between devices  235 us (57%)
  starting transfers between devices  95.7 us (23%)
  blocking collectives  38.7 us (9%)
  local copies, waits for them, and re-layouts  17.4 us (4%)
  between operations  14.6 us (4%)
  matrix products  7.68 us (2%)
    unnamed x5, waiting for transfers between devices  169 us
    ppermute x7, starting transfers between devices, ring_gather(): lax.ppermute(going_down, axis, [(d, (d - 1) % ways) for d in range(ways)])  50.6 us
    psum x1, blocking collectives, per_device(): grad_gates = lax.psum(partial_dots, ('pipe', 'tensor'))  38.7 us
    all_to_all x1, waiting for transfers between devices, per_device(): lax.all_to_all(send, 'expert', split_axis=0, concat_axis=0, tiled=True)  26.6 us
    all_to_all x1, waiting for transfers between devices, per_device(): lax.all_to_all(back_send, 'expert', split_axis=0, concat_axis=0, tiled=True)  26.5 us
    ppermute x8, starting transfers between devices, ring_gather(): lax.ppermute(going_up, axis, [(d, (d + 1) % ways) for d in range(ways)])  16.8 us
    all_to_all x1, starting transfers between devices, per_device(): lax.all_to_all(send, 'expert', split_axis=0, concat_axis=0, tiled=True)  15.3 us
    all_to_all x1, starting transfers between devices, per_device(): lax.all_to_all(back_send, 'expert', split_axis=0, concat_axis=0, tiled=True)  12.8 us
  transfers between devices with their start and end apart: 20, of which 15 were waited for; matrix products, arithmetic and copies ran while one was open for 4% of the time, Pallas kernels for 0%

profile of v1, /device:TPU:32, one launch (start us, length us, event | category | flops | bytes accessed | tf_op | source)
XLA Modules:
  0.0 412.7 jit_solution(5385787165078352291)
XLA Ops:
  7.2 0.9 copy.35
  8.3 0.2 select_reduce_fusion.1
  8.6 0.7 multiply_add_fusion
  9.3 0.8 convert_reduce_fusion
  10.1 0.9 convolution_convert_fusion.1
  11.0 0.9 convolution_convert_fusion.2
  12.0 0.8 broadcast_in_dim.5
  12.8 15.3 %all-to-all-start = ((bf16[32,5,768]{2,1,0:T(8,128)(2,1)}), bf16[32,5,768]{2,1,0:T(8,128)(2,1)S(1)}, u32[]{:S(2)}, u32[]{:S(2)}) async-start(bf16[32,5,768]{2,1,0:T(8,128)(2,1)} %bitcast), calls=%async_computation | async-start | bytes 786432 | tf_op jit(solution)/shard_map/all_to_all | solution.py:51
  28.2 26.6 %all-to-all-done = bf16[32,5,768]{2,1,0:T(8,128)(2,1)S(1)} async-done(((bf16[32,5,768]{2,1,0:T(8,128)(2,1)}), bf16[32,5,768]{2,1,0:T(8,128)(2,1)S(1)}, u32[]{:S(2)}, u32[]{:S(2)}) %all-to-all-start) | async-done | bytes 245792 | tf_op jit(solution)/shard_map/all_to_all | solution.py:51
  54.8 0.8 reshape.66
  55.6 0.2 broadcast_in_dim.4
  55.8 0.7 copy-done.8
  56.6 0.7 fusion.21
  57.4 3.4 collective-permute-start
  60.8 5.8 %collective-permute-start.1 = (bf16[160,384]{1,0:T(8,128)(2,1)}, bf16[160,384]{1,0:T(8,128)(2,1)}, u32[]{:S(2)}, u32[]{:S(2)}) collective-permute-start(bf16[160,384]{1,0:T(8,128)(2,1)} %get-tuple-element.22), channel_id=1, source_target_pairs={{0,387},{1,0},{2,1},{3,2},{128,3},{129,128},{130,129},{131,130},{2... | collective-permute-start | bytes 368648 | tf_op jit(solution)/shard_map/ppermute | solution.py:18
  66.8 0.9 collective-permute-done
  67.8 1.9 collective-permute-start.2
  69.7 0.2 collective-permute-done.1
  69.9 7.8 %collective-permute-start.3 = (bf16[160,384]{1,0:T(8,128)(2,1)}, bf16[160,384]{1,0:T(8,128)(2,1)S(1)}, u32[]{:S(2)}, u32[]{:S(2)}) collective-permute-start(bf16[160,384]{1,0:T(8,128)(2,1)} %collective-permute-done.1), channel_id=1, source_target_pairs={{0,387},{1,0},{2,1},{3,2},{128,3},{129,128},{130,129},{131,130},{2... | collective-permute-start | bytes 368648 | tf_op jit(solution)/shard_map/ppermute | solution.py:18
  77.7 0.9 constant_dynamic-update-slice_fusion.13
  78.6 0.9 constant_dynamic-update-slice_fusion.12
  79.5 1.9 collective-permute-start.4
  81.5 7.2 %collective-permute-start.5 = (bf16[160,384]{1,0:T(8,128)(2,1)S(1)}, bf16[160,384]{1,0:T(8,128)(2,1)S(1)}, u32[]{:S(2)}, u32[]{:S(2)}) collective-permute-start(bf16[160,384]{1,0:T(8,128)(2,1)S(1)} %collective-permute-done.3), channel_id=1, source_target_pairs={{0,387},{1,0},{2,1},{3,2},{128,3},{129,128},{130,129},{131,130},{2... | collective-permute-start | bytes 368648 | tf_op jit(solution)/shard_map/ppermute | solution.py:18
  88.8 0.8 collective-permute-done.4
  89.6 1.9 collective-permute-start.6
  91.6 7.2 %collective-permute-start.7 = (bf16[160,384]{1,0:T(8,128)(2,1)S(1)}, bf16[160,384]{1,0:T(8,128)(2,1)S(1)}, u32[]{:S(2)}, u32[]{:S(2)}) collective-permute-start(bf16[160,384]{1,0:T(8,128)(2,1)S(1)} %collective-permute-done.5), channel_id=1, source_target_pairs={{0,387},{1,0},{2,1},{3,2},{128,3},{129,128},{130,129},{131,130},{2... | collective-permute-start | bytes 368648 | tf_op jit(solution)/shard_map/ppermute | solution.py:18
  98.9 0.8 collective-permute-done.6
  99.7 1.9 collective-permute-start.8
  101.7 7.2 %collective-permute-start.9 = (bf16[160,384]{1,0:T(8,128)(2,1)S(1)}, bf16[160,384]{1,0:T(8,128)(2,1)S(1)}, u32[]{:S(2)}, u32[]{:S(2)}) collective-permute-start(bf16[160,384]{1,0:T(8,128)(2,1)S(1)} %collective-permute-done.7), channel_id=1, source_target_pairs={{0,387},{1,0},{2,1},{3,2},{128,3},{129,128},{130,129},{131,130},{2... | collective-permute-start | bytes 368648 | tf_op jit(solution)/shard_map/ppermute | solution.py:18
  109.0 1.7 collective-permute-done.8
  110.7 1.9 collective-permute-start.10
  112.6 0.2 collective-permute-done.9
  112.8 7.7 %collective-permute-start.11 = (bf16[160,384]{1,0:T(8,128)(2,1)S(1)}, bf16[160,384]{1,0:T(8,128)(2,1)S(1)}, u32[]{:S(2)}, u32[]{:S(2)}) collective-permute-start(bf16[160,384]{1,0:T(8,128)(2,1)S(1)} %collective-permute-done.9), channel_id=1, source_target_pairs={{0,387},{1,0},{2,1},{3,2},{128,3},{129,128},{130,129},{131,130},{2... | collective-permute-start | bytes 368648 | tf_op jit(solution)/shard_map/ppermute | solution.py:18
  120.6 0.2 collective-permute-done.10
  120.8 1.9 collective-permute-start.12
  122.7 0.3 collective-permute-done.11
  122.9 7.7 %collective-permute-start.13 = (bf16[160,384]{1,0:T(8,128)(2,1)S(1)}, bf16[160,384]{1,0:T(8,128)(2,1)S(1)}, u32[]{:S(2)}, u32[]{:S(2)}) collective-permute-start(bf16[160,384]{1,0:T(8,128)(2,1)S(1)} %collective-permute-done.11), channel_id=1, source_target_pairs={{0,387},{1,0},{2,1},{3,2},{128,3},{129,128},{130,129},{131,130},{2... | collective-permute-start | bytes 368648 | tf_op jit(solution)/shard_map/ppermute | solution.py:18
  130.7 0.2 collective-permute-done.12
  130.8 1.9 collective-permute-start.14
  132.8 0.2 collective-permute-done.13
  133.1 7.9 %collective-permute-done.14 = bf16[160,384]{1,0:T(8,128)(2,1)S(1)} collective-permute-done((bf16[160,384]{1,0:T(8,128)(2,1)S(1)}, bf16[160,384]{1,0:T(8,128)(2,1)S(1)}, u32[]{:S(2)}, u32[]{:S(2)}) %collective-permute-start.14) | collective-permute-done | bytes 122912 | tf_op jit(solution)/shard_map/ppermute | solution.py:15
  141.0 0.7 fusion.5
  141.6 0.7 fusion.9
  142.3 0.6 copy-done.5
  143.0 0.7 convolution_convert_fusion
  143.6 2.7 copy.38
  146.5 2.3 fusion.1
  148.9 0.7 fusion.7
  149.6 0.7 copy-done.4
  150.3 0.7 fusion
  151.0 2.7 copy.40
  153.8 74.9 %reduce-scatter.7.cloned.1.call-done = bf16[384,160]{1,0:T(8,128)(2,1)} async-done(((bf16[6144,160]{1,0:T(8,128)(2,1)}), bf16[384,160]{1,0:T(8,128)(2,1)}) %reduce-scatter.7.cloned.1.call-update) | async-done | bytes 122896
  228.7 1.1 copy.39
  229.8 93.6 %reduce-scatter.9.cloned.1.call-done = bf16[384,160]{1,0:T(8,128)(2,1)} async-done(((bf16[6144,160]{1,0:T(8,128)(2,1)}), bf16[384,160]{1,0:T(8,128)(2,1)}) %reduce-scatter.9.cloned.1.call-update) | async-done | bytes 122896
  323.4 1.1 copy.41
  324.5 0.8 reshape.67
  325.3 12.8 %all-to-all-start.1 = ((bf16[32,5,768]{2,1,0:T(8,128)(2,1)}), bf16[32,5,768]{2,1,0:T(8,128)(2,1)S(1)}, u32[]{:S(2)}, u32[]{:S(2)}) async-start(bf16[32,5,768]{2,1,0:T(8,128)(2,1)} %reshape.67), calls=%async_computation.1 | async-start | bytes 786432 | tf_op jit(solution)/shard_map/all_to_all | solution.py:86
  338.3 26.5 %all-to-all-done.1 = bf16[32,5,768]{2,1,0:T(8,128)(2,1)S(1)} async-done(((bf16[32,5,768]{2,1,0:T(8,128)(2,1)}), bf16[32,5,768]{2,1,0:T(8,128)(2,1)S(1)}, u32[]{:S(2)}, u32[]{:S(2)}) %all-to-all-start.1) | async-done | bytes 245792 | tf_op jit(solution)/shard_map/all_to_all | solution.py:86
  365.0 0.2 fusion.15
  365.1 0.1 multiply_reduce_fusion
  365.4 38.7 %psum.7 = f32[16,2]{1,0:T(8,128)S(1)} all-reduce(f32[16,2]{1,0:T(8,128)S(1)} %reduce_sum.72), channel_id=1, replica_groups=mesh['pipe'=4,'expert'=32,'tensor'=4] {'pipe','tensor'}, use_global_device_ids=true, to_apply=%region_10.11 | all-reduce | flops 32 | bytes 256 | tf_op jit(solution)/shard_map/psum | solution.py:99
  404.1 0.6 copy.37
  404.7 0.7 multiply_reduce_fusion.1
  405.5 0.7 reduce_sum.70
  (64 shorter events, 1.4 us)
Async XLA Ops:
  7.2 135.8 %copy-start = (bf16[1,128,6144]{2,1,0:T(8,128)(2,1)S(1)}, bf16[1,128,6144]{2,1,0:T(8,128)(2,1)}, u32[]{:S(2)}) copy-start(bf16[1,128,6144]{2,1,0:T(8,128)(2,1)} %param.12) | copy-start | bytes 4718596
  12.8 42.1 %all-to-all-start = ((bf16[32,5,768]{2,1,0:T(8,128)(2,1)}), bf16[32,5,768]{2,1,0:T(8,128)(2,1)S(1)}, u32[]{:S(2)}, u32[]{:S(2)}) async-start(bf16[32,5,768]{2,1,0:T(8,128)(2,1)} %bitcast), calls=%async_computation | async-start | bytes 786432 | tf_op jit(solution)/shard_map/all_to_all | solution.py:51
  28.1 118.4 %all-gather.2.cloned.1.call-start = ((), (), s32[]{:S(2)}) async-start(), calls=%async_computation.4 | async-start | bytes 2088960 | tf_op jit(solution)/shard_map/all_gather | solution.py:56
  55.6 0.9 copy-start.8
  57.3 171.4 %reduce-scatter.7.cloned.1.call-start = ((), (), s32[]{:S(2)}) async-start(), calls=%async_computation.5 | async-start | bytes 3342336
  57.4 10.4 %collective-permute-start = (bf16[160,384]{1,0:T(8,128)(2,1)}, bf16[160,384]{1,0:T(8,128)(2,1)}, u32[]{:S(2)}, u32[]{:S(2)}) collective-permute-start(bf16[160,384]{1,0:T(8,128)(2,1)} %get-tuple-element.22), channel_id=1, source_target_pairs={{0,1},{1,2},{2,3},{3,128},{128,129},{129,130},{130,131},{131,256},... | collective-permute-start | bytes 368648 | tf_op jit(solution)/shard_map/ppermute | solution.py:15
  60.8 9.1 %collective-permute-start.1 = (bf16[160,384]{1,0:T(8,128)(2,1)}, bf16[160,384]{1,0:T(8,128)(2,1)}, u32[]{:S(2)}, u32[]{:S(2)}) collective-permute-start(bf16[160,384]{1,0:T(8,128)(2,1)} %get-tuple-element.22), channel_id=1, source_target_pairs={{0,387},{1,0},{2,1},{3,2},{128,3},{129,128},{130,129},{131,130},{2... | collective-permute-start | bytes 368648 | tf_op jit(solution)/shard_map/ppermute | solution.py:18
  66.8 74.1 %copy-start.3 = (bf16[1,6144,128]{2,1,0:T(8,128)(2,1)S(1)}, bf16[1,6144,128]{2,1,0:T(8,128)(2,1)}, u32[]{:S(2)}) copy-start(bf16[1,6144,128]{2,1,0:T(8,128)(2,1)} %param.11) | copy-start | bytes 4718596
  67.8 11.8 %collective-permute-start.2 = (bf16[160,384]{1,0:T(8,128)(2,1)}, bf16[160,384]{1,0:T(8,128)(2,1)S(1)}, u32[]{:S(2)}, u32[]{:S(2)}) collective-permute-start(bf16[160,384]{1,0:T(8,128)(2,1)} %collective-permute-done), channel_id=1, source_target_pairs={{0,1},{1,2},{2,3},{3,128},{128,129},{129,130},{130,131},{131,256},... | collective-permute-start | bytes 368648 | tf_op jit(solution)/shard_map/ppermute | solution.py:15
  69.9 11.6 %collective-permute-start.3 = (bf16[160,384]{1,0:T(8,128)(2,1)}, bf16[160,384]{1,0:T(8,128)(2,1)S(1)}, u32[]{:S(2)}, u32[]{:S(2)}) collective-permute-start(bf16[160,384]{1,0:T(8,128)(2,1)} %collective-permute-done.1), channel_id=1, source_target_pairs={{0,387},{1,0},{2,1},{3,2},{128,3},{129,128},{130,129},{131,130},{2... | collective-permute-start | bytes 368648 | tf_op jit(solution)/shard_map/ppermute | solution.py:18
  79.5 10.1 %collective-permute-start.4 = (bf16[160,384]{1,0:T(8,128)(2,1)S(1)}, bf16[160,384]{1,0:T(8,128)(2,1)S(1)}, u32[]{:S(2)}, u32[]{:S(2)}) collective-permute-start(bf16[160,384]{1,0:T(8,128)(2,1)S(1)} %collective-permute-done.2), channel_id=1, source_target_pairs={{0,1},{1,2},{2,3},{3,128},{128,129},{129,130},{130,131},{131,256},... | collective-permute-start | bytes 368648 | tf_op jit(solution)/shard_map/ppermute | solution.py:15
  81.5 10.1 %collective-permute-start.5 = (bf16[160,384]{1,0:T(8,128)(2,1)S(1)}, bf16[160,384]{1,0:T(8,128)(2,1)S(1)}, u32[]{:S(2)}, u32[]{:S(2)}) collective-permute-start(bf16[160,384]{1,0:T(8,128)(2,1)S(1)} %collective-permute-done.3), channel_id=1, source_target_pairs={{0,387},{1,0},{2,1},{3,2},{128,3},{129,128},{130,129},{131,130},{2... | collective-permute-start | bytes 368648 | tf_op jit(solution)/shard_map/ppermute | solution.py:18
  89.6 10.1 %collective-permute-start.6 = (bf16[160,384]{1,0:T(8,128)(2,1)S(1)}, bf16[160,384]{1,0:T(8,128)(2,1)S(1)}, u32[]{:S(2)}, u32[]{:S(2)}) collective-permute-start(bf16[160,384]{1,0:T(8,128)(2,1)S(1)} %collective-permute-done.4), channel_id=1, source_target_pairs={{0,1},{1,2},{2,3},{3,128},{128,129},{129,130},{130,131},{131,256},... | collective-permute-start | bytes 368648 | tf_op jit(solution)/shard_map/ppermute | solution.py:15
  91.6 10.1 %collective-permute-start.7 = (bf16[160,384]{1,0:T(8,128)(2,1)S(1)}, bf16[160,384]{1,0:T(8,128)(2,1)S(1)}, u32[]{:S(2)}, u32[]{:S(2)}) collective-permute-start(bf16[160,384]{1,0:T(8,128)(2,1)S(1)} %collective-permute-done.5), channel_id=1, source_target_pairs={{0,387},{1,0},{2,1},{3,2},{128,3},{129,128},{130,129},{131,130},{2... | collective-permute-start | bytes 368648 | tf_op jit(solution)/shard_map/ppermute | solution.py:18
  99.7 10.9 %collective-permute-start.8 = (bf16[160,384]{1,0:T(8,128)(2,1)S(1)}, bf16[160,384]{1,0:T(8,128)(2,1)S(1)}, u32[]{:S(2)}, u32[]{:S(2)}) collective-permute-start(bf16[160,384]{1,0:T(8,128)(2,1)S(1)} %collective-permute-done.6), channel_id=1, source_target_pairs={{0,1},{1,2},{2,3},{3,128},{128,129},{129,130},{130,131},{131,256},... | collective-permute-start | bytes 368648 | tf_op jit(solution)/shard_map/ppermute | solution.py:15
  101.7 11.2 %collective-permute-start.9 = (bf16[160,384]{1,0:T(8,128)(2,1)S(1)}, bf16[160,384]{1,0:T(8,128)(2,1)S(1)}, u32[]{:S(2)}, u32[]{:S(2)}) collective-permute-start(bf16[160,384]{1,0:T(8,128)(2,1)S(1)} %collective-permute-done.7), channel_id=1, source_target_pairs={{0,387},{1,0},{2,1},{3,2},{128,3},{129,128},{130,129},{131,130},{2... | collective-permute-start | bytes 368648 | tf_op jit(solution)/shard_map/ppermute | solution.py:18
  110.7 10.1 %collective-permute-start.10 = (bf16[160,384]{1,0:T(8,128)(2,1)S(1)}, bf16[160,384]{1,0:T(8,128)(2,1)S(1)}, u32[]{:S(2)}, u32[]{:S(2)}) collective-permute-start(bf16[160,384]{1,0:T(8,128)(2,1)S(1)} %collective-permute-done.8), channel_id=1, source_target_pairs={{0,1},{1,2},{2,3},{3,128},{128,129},{129,130},{130,131},{131,256},... | collective-permute-start | bytes 368648 | tf_op jit(solution)/shard_map/ppermute | solution.py:15
  112.8 10.1 %collective-permute-start.11 = (bf16[160,384]{1,0:T(8,128)(2,1)S(1)}, bf16[160,384]{1,0:T(8,128)(2,1)S(1)}, u32[]{:S(2)}, u32[]{:S(2)}) collective-permute-start(bf16[160,384]{1,0:T(8,128)(2,1)S(1)} %collective-permute-done.9), channel_id=1, source_target_pairs={{0,387},{1,0},{2,1},{3,2},{128,3},{129,128},{130,129},{131,130},{2... | collective-permute-start | bytes 368648 | tf_op jit(solution)/shard_map/ppermute | solution.py:18
  120.8 10.1 %collective-permute-start.12 = (bf16[160,384]{1,0:T(8,128)(2,1)S(1)}, bf16[160,384]{1,0:T(8,128)(2,1)S(1)}, u32[]{:S(2)}, u32[]{:S(2)}) collective-permute-start(bf16[160,384]{1,0:T(8,128)(2,1)S(1)} %collective-permute-done.10), channel_id=1, source_target_pairs={{0,1},{1,2},{2,3},{3,128},{128,129},{129,130},{130,131},{131,256},... | collective-permute-start | bytes 368648 | tf_op jit(solution)/shard_map/ppermute | solution.py:15
  122.9 10.1 %collective-permute-start.13 = (bf16[160,384]{1,0:T(8,128)(2,1)S(1)}, bf16[160,384]{1,0:T(8,128)(2,1)S(1)}, u32[]{:S(2)}, u32[]{:S(2)}) collective-permute-start(bf16[160,384]{1,0:T(8,128)(2,1)S(1)} %collective-permute-done.11), channel_id=1, source_target_pairs={{0,387},{1,0},{2,1},{3,2},{128,3},{129,128},{130,129},{131,130},{2... | collective-permute-start | bytes 368648 | tf_op jit(solution)/shard_map/ppermute | solution.py:18
  130.8 10.1 %collective-permute-start.14 = (bf16[160,384]{1,0:T(8,128)(2,1)S(1)}, bf16[160,384]{1,0:T(8,128)(2,1)S(1)}, u32[]{:S(2)}, u32[]{:S(2)}) collective-permute-start(bf16[160,384]{1,0:T(8,128)(2,1)S(1)} %collective-permute-done.12), channel_id=1, source_target_pairs={{0,1},{1,2},{2,3},{3,128},{128,129},{129,130},{130,131},{131,256},... | collective-permute-start | bytes 368648 | tf_op jit(solution)/shard_map/ppermute | solution.py:15
  133.1 8.6 %copy-start.1 = (bf16[1,6144,128]{2,1,0:T(8,128)(2,1)S(1)}, bf16[1,6144,128]{2,1,0:T(8,128)(2,1)}, u32[]{:S(2)}) copy-start(bf16[1,6144,128]{2,1,0:T(8,128)(2,1)} %param.10) | copy-start | bytes 4718596
  141.6 0.7 copy-start.9
  142.3 0.6 copy-start.5
  146.4 2.4 copy-start.2
  146.4 2.4 copy-start.6
  146.4 2.4 copy-start.10
  146.4 176.9 %reduce-scatter.9.cloned.1.call-start = ((), (), s32[]{:S(2)}) async-start(), calls=%async_computation.6 | async-start | bytes 3342336
  148.9 1.4 copy-start.4
  148.9 1.4 copy-start.7
  153.7 184.4 %copy-start.12 = (f32[16,2]{0,1:T(2,128)S(1)}, f32[16,2]{0,1:T(2,128)}, u32[]{:S(2)}) copy-start(f32[16,2]{0,1:T(2,128)} %param.9) | copy-start | bytes 388
  153.8 184.5 %copy-start.11 = (bf16[16,384]{1,0:T(8,128)(2,1)S(1)}, bf16[16,384]{1,0:T(8,128)(2,1)}, u32[]{:S(2)}) copy-start(bf16[16,384]{1,0:T(8,128)(2,1)} %param.13) | copy-start | bytes 36868
  325.3 39.5 %all-to-all-start.1 = ((bf16[32,5,768]{2,1,0:T(8,128)(2,1)}), bf16[32,5,768]{2,1,0:T(8,128)(2,1)S(1)}, u32[]{:S(2)}, u32[]{:S(2)}) async-start(bf16[32,5,768]{2,1,0:T(8,128)(2,1)} %reshape.67), calls=%async_computation.1 | async-start | bytes 786432 | tf_op jit(solution)/shard_map/all_to_all | solution.py:86
Sparse Core Ops, SparseCore 0:
  57.4 59.3 all-gather.1
  146.5 82.1 reduce-scatter.6
  232.9 90.4 reduce-scatter.8
